TPU v7x, 128 devices: a whole 4x4x4 slice. The times are simulated.
128 devices in a mesh: grp: 4 (over y_lo, core), band: 32 (over y_hi, x, z).
Axes of the slice: x: 4, y: 4 (y_hi: 2, y_lo: 2; y = y_hi * 2 + y_lo), z: 4, core: 2. Of those that a mesh axis runs over, the one named last changes fastest.
Arguments:
- prior_samples: bfloat16 [32, 69, 64, 1024], P('grp', None, 'band'), may hold values from -6 to 6
- conv1_weight: bfloat16 [3, 3, 256, 69], replicated, may hold values from -0.25 to 0.25
- conv1_bias: float32 [256], replicated, may hold values from -3 to 3
- conv2_weight: bfloat16 [3, 3, 69, 256], replicated, may hold values from -0.125 to 0.125
- conv2_bias: float32 [69], replicated, may hold values from -3 to 3
- obs_index: int32 [256, 256], P(('grp', 'band')), may hold values from 0 to 17663
- obs_values: float32 [256, 256], P(('grp', 'band')), may hold values from -6 to 6
- obs_prec: float32 [256, 256], P(('grp', 'band')), may hold values from 0.25 to 4
- neighbours: int32 [256, 8], P(('grp', 'band')), may hold values from 0 to 255
- loc_weight: float32 [256, 8], P(('grp', 'band')), may hold values from 0.2 to 1
Outputs:
- analysis: float32 [32, 69, 64, 1024], P(None, None, 'band', 'grp')
Inputs may be any that keep to these rules, and one draw needn't show every extreme that they name: `neighbours`: neighbour patch numbers; a number may repeat or name the patch itself. `obs_index`: observed entry as channel * 256 + column within the patch.
All inputs are finite; a program needn't handle non-finite values.
Results may differ from a plain program's by a relative error of at most 0.0021.
Values may be sent and summed in bfloat16 or wider, within the bound.
No kernel may reach another device: no remote copies, remote signals or barrier semaphores. Data moves between devices by JAX's collectives and lax.ppermute only.
A program may use at most 128 MiB of HBM per device.

v0:
```python
import jax
import jax.numpy as jnp
from jax import lax
from jax.sharding import PartitionSpec as P

NS_ITERS = 6


def padded_2(cells, sides, width):
    for axis, dim in sides:
        count = lax.axis_size(axis)
        ends = count - 1
        head = lax.slice_in_dim(cells, 0, width, axis=dim)
        tail = lax.slice_in_dim(cells, cells.shape[dim] - width, cells.shape[dim], axis=dim)
        cells = jnp.concatenate(
            [
                lax.ppermute(tail, axis, [(i, (i + 1) % count) for i in range(ends)]),
                cells,
                lax.ppermute(head, axis, [((i + 1) % count, i) for i in range(ends)]),
            ],
            axis=dim,
        )
    return cells


def from_behind(block, axis, distance):
    devices = range(lax.axis_size(axis))
    route = [(i - distance, i) for i in devices if i - distance in devices]
    return lax.ppermute(block, axis, route)


def convolve(padded, kernel, height):
    summed = jnp.zeros((kernel.shape[2], height, padded.shape[2]), jnp.float32)
    for row_shift in range(3):
        window = padded[:, row_shift : row_shift + height, :]
        for col_shift in range(3):
            shifted = jnp.roll(window, 1 - col_shift, axis=2)
            summed = summed + jnp.einsum(
                "oc,crl->orl",
                kernel[row_shift, col_shift],
                shifted,
                preferred_element_type=jnp.float32,
            )
    return summed


def grams_of(perturb, obs_prec, innovation):
    highest = lax.Precision.HIGHEST
    gram_local = jnp.einsum("pmo,po,pno->pmn", perturb, obs_prec, perturb, precision=highest)
    pull_vec = jnp.einsum("pmo,po->pm", perturb, obs_prec * innovation, precision=highest)
    return (gram_local, pull_vec)


def on_device(
    prior_samples,
    conv1_weight,
    conv1_bias,
    conv2_weight,
    conv2_bias,
    obs_index,
    obs_values,
    obs_prec,
    neighbours,
    loc_weight,
):
    highest = lax.Precision.HIGHEST
    height = prior_samples.shape[2]
    padded = padded_2(prior_samples, (("band", 2),), 1)

    def first_layer(member):
        return jax.nn.silu(
            convolve(member, conv1_weight, height) + conv1_bias[:, None, None]
        ).astype(jnp.bfloat16)

    hidden_fields = lax.map(first_layer, padded)
    northern_halo = from_behind(hidden_fields[:, :, height - 1 :, :], "band", 1)
    southern_halo = from_behind(hidden_fields[:, :, :1, :], "band", -1)

    def output_layer(inputs):
        member, own_rows, above_row, below_row = inputs
        extended = jnp.concatenate([above_row, own_rows, below_row], axis=1)
        summed = (
            member.astype(jnp.float32)
            + convolve(extended, conv2_weight, height)
            + conv2_bias[:, None, None]
        )
        return summed.astype(jnp.bfloat16)

    predicted_samples = lax.map(
        output_layer, (prior_samples, hidden_fields, northern_halo, southern_halo)
    )
    patch_block_slice = lax.all_to_all(
        predicted_samples, "grp", split_axis=3, concat_axis=0, tiled=True
    )
    ensemble = patch_block_slice.shape[0]
    channels = patch_block_slice.shape[1]
    patch_width = patch_block_slice.shape[3]
    realization_grid = jnp.transpose(patch_block_slice, (2, 0, 1, 3)).reshape(
        height, ensemble, channels * patch_width
    )
    count_obs = obs_index.shape[1]
    chosen = jnp.broadcast_to(obs_index[:, None, :], (height, ensemble, count_obs))
    predicted = jnp.take_along_axis(realization_grid, chosen, axis=2).astype(jnp.float32)
    predicted_mean = jnp.mean(predicted, axis=1)
    perturb = predicted - predicted_mean[:, None, :]
    innovation = obs_values - predicted_mean
    gram_local, pull_vec = grams_of(perturb, obs_prec, innovation)
    total_patches = height * lax.axis_size("grp") * lax.axis_size("band")
    patch_ids = jnp.arange(total_patches, dtype=jnp.int32)
    matches = (neighbours[:, :, None] == patch_ids[None, None, :]).astype(jnp.float32)
    spread_weights = jnp.sum(loc_weight[:, :, None] * matches, axis=1)
    piece_gram, piece_pull = grams_of(
        lax.all_gather(perturb, ("grp", "band"), axis=0, tiled=True),
        lax.all_gather(obs_prec, ("grp", "band"), axis=0, tiled=True),
        lax.all_gather(innovation, ("grp", "band"), axis=0, tiled=True),
    )
    gram_sum = jnp.einsum("pj,jab->pab", spread_weights, piece_gram, precision=highest)
    pull_sum = jnp.einsum("pj,ja->pa", spread_weights, piece_pull, precision=highest)
    identity = jnp.broadcast_to(jnp.eye(ensemble, dtype=jnp.float32), (height, ensemble, ensemble))
    matrix = (ensemble - 1.0) * identity + gram_local + gram_sum
    pulled = pull_vec + pull_sum
    norm_scale = jnp.sqrt(jnp.sum(matrix * matrix, axis=(1, 2)))
    sqrt_iter = matrix / norm_scale[:, None, None]
    inverse_root = identity
    for sweep in range(NS_ITERS):
        half_step = 1.5 * identity - 0.5 * jnp.einsum(
            "pab,pbc->pac", inverse_root, sqrt_iter, precision=highest
        )
        sqrt_iter = jnp.einsum("pab,pbc->pac", sqrt_iter, half_step, precision=highest)
        inverse_root = jnp.einsum("pab,pbc->pac", half_step, inverse_root, precision=highest)
    once_applied = jnp.einsum("pab,pb->pa", inverse_root, pulled, precision=highest)
    mean_weight = (
        jnp.einsum("pab,pb->pa", inverse_root, once_applied, precision=highest)
        / norm_scale[:, None]
    )
    transform = (jnp.sqrt(ensemble - 1.0) / jnp.sqrt(norm_scale))[
        :, None, None
    ] * inverse_root + mean_weight[:, :, None]
    field = realization_grid.astype(jnp.float32)
    centre = jnp.mean(field, axis=1)
    spread = field - centre[:, None, :]
    analysed = centre[:, None, :] + jnp.einsum("pkm,pkc->pmc", transform, spread, precision=highest)
    return analysed.reshape(height, ensemble, channels, patch_width).transpose(1, 2, 0, 3)


def solution(mesh):
    placed = (
        P("grp", None, "band", None),
        P(),
        P(),
        P(),
        P(),
        P(("grp", "band"), None),
        P(("grp", "band"), None),
        P(("grp", "band"), None),
        P(("grp", "band"), None),
        P(("grp", "band"), None),
    )
    return jax.shard_map(
        on_device,
        mesh=mesh,
        in_specs=placed,
        out_specs=P(None, None, "band", "grp"),
        check_vma=False,
    )
```

profile of v0, /device:TPU:48, one launch (start us, length us, event | category | flops | bytes accessed | tf_op | source)
XLA Modules:
  0.0 1311.0 jit_solution(5187582412730233797)
XLA Ops:
  6.5 5.9 fusion.156
  12.9 4.0 collective-permute-start
  16.9 1.4 copy.95
  18.3 2.0 collective-permute-start.1
  21.0 20.6 %collective-permute-done = bf16[8,69,1,1024]{3,0,2,1:T(8,128)(2,1)} collective-permute-done((bf16[8,69,1,1024]{3,0,2,1:T(8,128)(2,1)S(1)}, bf16[8,69,1,1024]{3,0,2,1:T(8,128)(2,1)}, u32[]{:S(2)}, u32[]{:S(2)}) %collective-permute-start) | collective-permute-done | bytes 1130528 | tf_op jit(solution)/shard_map/ppermute | solution.py:17
  41.7 1.9 copy.66
  43.6 3.3 collective-permute-done.1
  46.8 1.9 copy.68
  48.7 2.5 pad_maximum_fusion.6
  51.3 73.3 %while.20 = (s32[]{:T(128)}, bf16[8,256,2,1024]{3,1,2,0:T(8,128)(2,1)}, bf16[8,69,4,1024]{3,1,2,0:T(8,128)(2,1)}, bf16[3,3,256,69]{2,3,1,0:T(8,128)(2,1)S(1)}, f32[256]{0:T(256)S(1)}, /*index=5*/s32[]{:T(128)}) while((s32[]{:T(128)}, bf16[8,256,2,1024]{3,1,2,0:T(8,128)(2,1)}, bf16[8,69,4,1024]{3,1,2,0:T(8,128)(2,1)}, ...), condition=%wide.region_1.2_spmd, body=%wide.region_0.1_spmd.sunk | while | flops 661897216 | bytes 47412808 | solution.py:75
  124.5 6.1 fusion.155
  130.6 3.5 collective-permute-start.2
  134.1 4.2 collective-permute-start.3
  138.4 87.3 %collective-permute-done.2 = bf16[8,256,1,1024]{3,1,2,0:T(8,128)(2,1)} collective-permute-done((bf16[8,256,1,1024]{3,1,2,0:T(8,128)(2,1)}, bf16[8,256,1,1024]{3,1,2,0:T(8,128)(2,1)}, u32[]{:S(2)}, u32[]{:S(2)}) %collective-permute-start.2) | collective-permute-done | bytes 4194336 | tf_op jit(solution)/shard_map/ppermute | solution.py:29
  225.7 2.4 collective-permute-done.3
  228.0 70.6 %while.21 = (s32[]{:T(128)}, bf16[8,69,2,1024]{3,1,2,0:T(8,128)(2,1)S(1)}, bf16[8,69,2,1024]{3,1,2,0:T(8,128)(2,1)}, bf16[8,256,1,1024]{3,1,2,0:T(8,128)(2,1)}, ...) while((s32[]{:T(128)}, ...), condition=%wide.region_3.4_spmd, body=%wide.region_2.3_spmd.sunk | while | flops 675929088 | bytes 41343592 | solution.py:89
  228.0 1.3 dynamic-slice_bitcast_fusion.9
  229.3 1.3 dynamic-slice_bitcast_fusion.8
  230.6 1.4 fusion.307
  235.6 1.3 fusion.310
  236.9 1.3 dynamic-slice_bitcast_fusion.9
  238.2 1.3 dynamic-slice_bitcast_fusion.8
  239.4 1.4 fusion.307
  244.4 1.3 fusion.310
  245.7 1.3 dynamic-slice_bitcast_fusion.9
  247.0 1.3 dynamic-slice_bitcast_fusion.8
  248.3 1.4 fusion.307
  253.2 1.3 fusion.310
  254.5 1.3 dynamic-slice_bitcast_fusion.9
  255.8 1.3 dynamic-slice_bitcast_fusion.8
  257.1 1.4 fusion.307
  262.0 1.3 fusion.310
  263.3 1.3 dynamic-slice_bitcast_fusion.9
  264.6 1.3 dynamic-slice_bitcast_fusion.8
  265.9 1.4 fusion.307
  270.9 1.3 fusion.310
  272.1 1.3 dynamic-slice_bitcast_fusion.9
  273.4 1.3 dynamic-slice_bitcast_fusion.8
  274.7 1.4 fusion.307
  279.7 1.3 fusion.310
  281.0 1.3 dynamic-slice_bitcast_fusion.9
  282.3 1.3 dynamic-slice_bitcast_fusion.8
  283.5 1.4 fusion.307
  288.5 1.3 fusion.310
  289.8 1.3 dynamic-slice_bitcast_fusion.9
  291.1 1.3 dynamic-slice_bitcast_fusion.8
  292.4 1.4 fusion.307
  297.3 1.3 fusion.310
  298.6 7.7 copy.73
  306.3 5.0 all-to-all-start
  311.4 48.1 %all-to-all-done = bf16[8,69,2,1024]{1,2,0,3:T(2,128)(2,1)} async-done(((bf16[8,69,2,1024]{1,2,0,3:T(2,128)(2,1)}), bf16[8,69,2,1024]{1,2,0,3:T(2,128)(2,1)}, u32[]{:S(2)}, u32[]{:S(2)}) %all-to-all-start) | async-done | bytes 2261024 | tf_op jit(solution)/shard_map/all_to_all | solution.py:92
  359.5 10.5 copy.90
  370.0 2.7 copy.91
  372.7 3.1 reshape.45
  375.9 159.3 %gather_fusion = bf16[16384]{0:T(1024)(128)(2,1)S(1)} fusion(bf16[2,32,17664]{2,1,0:T(8,128)(2,1)S(1)} %reshape.45, s32[16384]{0:T(1024)S(1)} %bitcast.273), kind=kCustom, calls=%fused_computation | custom fusion | bytes 262144 | tf_op jit(solution)/shard_map/jit(take_along_axis)/gather | solution.py:103
  535.9 356.6 %all-gather = f32[128,2,256]{2,1,0:T(2,128)S(1)} all-gather(f32[1,2,256]{2,1,0:T(2,128)S(1)} %bitcast.281), channel_id=1, replica_groups=mesh['grp'=4,'band'=32] {'grp','band'}, dimensions={0}, use_global_device_ids=true | all-gather | bytes 264192 | tf_op jit(solution)/shard_map/all_gather | solution.py:114
  892.8 356.1 %all-gather.1 = f32[128,2,256]{2,1,0:T(2,128)S(1)} all-gather(f32[1,2,256]{2,1,0:T(2,128)S(1)} %get-tuple-element.172), channel_id=1, replica_groups=mesh['grp'=4,'band'=32] {'grp','band'}, dimensions={0}, use_global_device_ids=true | all-gather | bytes 264192 | tf_op jit(solution)/shard_map/all_gather | solution.py:115
  1249.3 2.9 convert_reduce_fusion
  1252.3 14.7 %fusion.116 = f32[256,32,32]{2,1,0:T(8,128)S(1)} fusion(f32[256,32,256]{2,1,0:T(8,128)} %all-gather.4.cloned.1.call-done, f32[256,256]{1,0:T(8,128)S(1)} %reshape.55), kind=kOutput, calls=%fused_computation.146 | convolution fusion | flops 807403520 | bytes 9699328 | tf_op jit(solution)/shard_map/pmo,po,pno->pmn/dot_general | solution.py:49
  1267.0 4.3 fusion.120
  1274.7 9.9 fusion.131
  1285.2 5.6 convolution_add_fusion.7
  1290.8 5.1 reshape.46
  1296.0 7.9 copy.80
  (255 shorter events, 107.6 us)
Async XLA Ops:
  12.9 7.4 copy-start
  12.9 28.8 %collective-permute-start = (bf16[8,69,1,1024]{3,0,2,1:T(8,128)(2,1)S(1)}, bf16[8,69,1,1024]{3,0,2,1:T(8,128)(2,1)}, u32[]{:S(2)}, u32[]{:S(2)}) collective-permute-start(bf16[8,69,1,1024]{3,0,2,1:T(8,128)(2,1)S(1)} %copy.94), channel_id=1, source_target_pairs={{0,1},{1,2},{2,3},{3,4},{4,5},{5,6},{6,7},{7,8},{8,9},{9,10},{10,1... | collective-permute-start | bytes 3391496 | tf_op jit(solution)/shard_map/ppermute | solution.py:17
  18.3 28.6 %collective-permute-start.1 = (bf16[8,69,1,1024]{3,0,2,1:T(8,128)(2,1)}, bf16[8,69,1,1024]{3,0,2,1:T(8,128)(2,1)}, u32[]{:S(2)}, u32[]{:S(2)}) collective-permute-start(bf16[8,69,1,1024]{3,0,2,1:T(8,128)(2,1)} %copy.95), channel_id=1, source_target_pairs={{1,0},{2,1},{3,2},{4,3},{5,4},{6,5},{7,6},{8,7},{9,8},{10,9},{11,1... | collective-permute-start | bytes 3391496 | tf_op jit(solution)/shard_map/ppermute | solution.py:19
  21.0 27.7 %copy-start.2 = (bf16[8,69,2,1024]{3,1,2,0:T(8,128)(2,1)}, bf16[8,69,2,1024]{3,1,2,0:T(8,128)(2,1)S(1)}, u32[]{:S(2)}) copy-start(bf16[8,69,2,1024]{3,1,2,0:T(8,128)(2,1)S(1)} %copy.71) | copy-start | bytes 6782980
  48.7 2.6 copy-start.3
  48.7 2.5 copy-start.6
  124.5 103.5 %copy-start.4 = (bf16[3,3,69,256]{3,2,1,0:T(8,128)(2,1)S(1)}, bf16[3,3,69,256]{3,2,1,0:T(8,128)(2,1)}, u32[]{:S(2)}) copy-start(bf16[3,3,69,256]{3,2,1,0:T(8,128)(2,1)} %param.17) | copy-start | bytes 953860
  124.5 103.5 %copy-start.11 = (f32[69]{0:T(128)S(1)}, f32[69]{0:T(128)}, u32[]{:S(2)}) copy-start(f32[69]{0:T(128)} %param.18) | copy-start | bytes 832
  130.6 95.0 %collective-permute-start.2 = (bf16[8,256,1,1024]{3,1,2,0:T(8,128)(2,1)}, bf16[8,256,1,1024]{3,1,2,0:T(8,128)(2,1)}, u32[]{:S(2)}, u32[]{:S(2)}) collective-permute-start(bf16[8,256,1,1024]{3,1,2,0:T(8,128)(2,1)} %get-tuple-element.169), channel_id=1, source_target_pairs={{0,1},{1,2},{2,3},{3,4},{4,5},{5,6},{6,7},{7,8},{8,9},{9,10},{10,1... | collective-permute-start | bytes 12582920 | tf_op jit(solution)/shard_map/ppermute | solution.py:29
  134.1 93.9 %collective-permute-start.3 = (bf16[8,256,1,1024]{3,1,2,0:T(8,128)(2,1)}, bf16[8,256,1,1024]{3,1,2,0:T(8,128)(2,1)}, u32[]{:S(2)}, u32[]{:S(2)}) collective-permute-start(bf16[8,256,1,1024]{3,1,2,0:T(8,128)(2,1)} %get-tuple-element.168), channel_id=1, source_target_pairs={{1,0},{2,1},{3,2},{4,3},{5,4},{6,5},{7,6},{8,7},{9,8},{10,9},{11,1... | collective-permute-start | bytes 12582920 | tf_op jit(solution)/shard_map/ppermute | solution.py:29
  306.3 5.0 copy-start.5
  306.3 53.2 %all-to-all-start = ((bf16[8,69,2,1024]{1,2,0,3:T(2,128)(2,1)}), bf16[8,69,2,1024]{1,2,0,3:T(2,128)(2,1)}, u32[]{:S(2)}, u32[]{:S(2)}) async-start(bf16[8,69,2,1024]{1,2,0,3:T(2,128)(2,1)} %copy.73), calls=%async_computation | async-start | bytes 8388608 | tf_op jit(solution)/shard_map/all_to_all | solution.py:92
  311.3 941.0 %all-gather.4.cloned.1.call-start = ((), (), s32[]{:S(2)}) async-start(), calls=%async_computation.1 | async-start | bytes 8454144 | tf_op jit(solution)/shard_map/all_gather | solution.py:113
  370.0 2.7 copy-start.1
  375.8 159.4 %copy-start.7 = (f32[2,256]{1,0:T(2,128)S(1)}, f32[2,256]{1,0:T(2,128)}, u32[]{:S(2)}) copy-start(f32[2,256]{1,0:T(2,128)} %param.21) | copy-start | bytes 6148
  375.8 159.4 %copy-start.8 = (f32[2,256]{1,0:T(2,128)S(1)}, f32[2,256]{1,0:T(2,128)}, u32[]{:S(2)}) copy-start(f32[2,256]{1,0:T(2,128)} %param.20) | copy-start | bytes 6148
  375.8 516.9 %copy-start.9 = (f32[2,8]{1,0:T(2,128)S(1)}, f32[2,8]{1,0:T(2,128)}, u32[]{:S(2)}) copy-start(f32[2,8]{1,0:T(2,128)} %param.23) | copy-start | bytes 196
  375.8 516.9 %copy-start.10 = (s32[2,8]{1,0:T(2,128)S(1)}, s32[2,8]{1,0:T(2,128)}, u32[]{:S(2)}) copy-start(s32[2,8]{1,0:T(2,128)} %param.22) | copy-start | bytes 196
Sparse Core Ops, SparseCore 0:
  536.0 320.7 all-gather.3
where the time goes:
time: 1320 us; the launch traced here: 1310 us
  blocking collectives  713 us (54%)
  local copies, waits for them, and re-layouts  261 us (20%)
  waiting for transfers between devices  162 us (12%)
  matrix products  123 us (9%)
  starting transfers between devices  18.7 us (1%)
  other arithmetic  18.6 us (1%)
  between operations  14.1 us (1%)
    all_gather x1, blocking collectives, on_device(): lax.all_gather(obs_prec, ('grp', 'band'), axis=0, tiled=True)  357 us
    all_gather x1, blocking collectives, on_device(): lax.all_gather(innovation, ('grp', 'band'), axis=0, tiled=True)  356 us
    gather x2, local copies, waits for them, and re-layouts, on_device(): jnp.take_along_axis(realization_grid, chosen, axis=2).astype(jnp.float32)  159 us
    ppermute x2, waiting for transfers between devices, from_behind(): return lax.ppermute(block, axis, route)  89.7 us
    dot_general x144, matrix products, convolve(): jnp.einsum('oc,crl->orl', kernel[row_shift, col_shift], shifted, preferre...  84.6 us
    all_to_all x1, waiting for transfers between devices, on_device(): lax.all_to_all(predicted_samples, 'grp', split_axis=3, concat_axis=0, til...  48.1 us
  transfers between devices with their start and end apart: 6, of which 5 were waited for; matrix products, arithmetic and copies ran while one was open for 1% of the time, Pallas kernels for 0%

commit v1 on v0

--- a/solution.py
+++ b/solution.py
@@ -111,7 +111,12 @@
     spread_weights = jnp.sum(loc_weight[:, :, None] * matches, axis=1)
     piece_gram, piece_pull = grams_of(
         lax.all_gather(perturb, ("grp", "band"), axis=0, tiled=True),
-        lax.all_gather(obs_prec, ("grp", "band"), axis=0, tiled=True),
+        jnp.concatenate(
+            lax.all_to_all(
+                jnp.stack([obs_prec] * lax.axis_size(("grp", "band"))), ("grp", "band"), 0, 0
+            ),
+            axis=0,
+        ),
         lax.all_gather(innovation, ("grp", "band"), axis=0, tiled=True),
     )
     gram_sum = jnp.einsum("pj,jab->pab", spread_weights, piece_gram, precision=highest)

time: 1320 us -> 996 us (0.75)
  blocking collectives: 713 us -> 350 us
  starting transfers between devices: 18.7 us -> 35.1 us
    all_gather x1 -> x0, blocking collectives: 357 us -> none  [on_device(): lax.all_gather(obs_prec, ('grp', 'band'), axis=0, tiled=True)]
    all_to_all x0 -> x1, starting transfers between devices: none -> 16.3 us  [on_device(): lax.all_to_all(jnp.stack([obs_prec] * lax.axis_size(('grp', 'band'))), ('...]
  transfers between devices with their start and end apart: 6 -> 7, of which waited for: 5 -> 6; matrix products, arithmetic and copies ran while one was open for 1% -> 1% of each run, Pallas kernels for 0% -> 0%
where the time goes in v1:
time: 996 us; the launch traced here: 984 us
  blocking collectives  350 us (35%)
  local copies, waits for them, and re-layouts  267 us (27%)
  waiting for transfers between devices  169 us (17%)
  matrix products  129 us (13%)
  starting transfers between devices  35.1 us (4%)
  other arithmetic  18.8 us (2%)
  between operations  14.1 us (1%)
    all_gather x1, blocking collectives, on_device(): lax.all_gather(innovation, ('grp', 'band'), axis=0, tiled=True)  350 us
    gather x2, local copies, waits for them, and re-layouts, on_device(): jnp.take_along_axis(realization_grid, chosen, axis=2).astype(jnp.float32)  159 us
    dot_general x144, matrix products, convolve(): jnp.einsum('oc,crl->orl', kernel[row_shift, col_shift], shifted, preferre...  90.8 us
    ppermute x2, waiting for transfers between devices, from_behind(): return lax.ppermute(block, axis, route)  89.7 us
    all_to_all x1, waiting for transfers between devices, on_device(): lax.all_to_all(predicted_samples, 'grp', split_axis=3, concat_axis=0, til...  48.1 us
    squeeze x16, local copies, waits for them, and re-layouts, on_device(): lax.map(output_layer, (prior_samples, hidden_fields, northern_halo, south...  20.5 us
  transfers between devices with their start and end apart: 7, of which 6 were waited for; matrix products, arithmetic and copies ran while one was open for 1% of the time, Pallas kernels for 0%

profile of v1, /device:TPU:48, one launch (start us, length us, event | category | flops | bytes accessed | tf_op | source)
XLA Modules:
  0.0 983.9 jit_solution(92971103019147899)
XLA Ops:
  6.5 6.0 fusion.156
  13.0 4.0 collective-permute-start
  17.0 1.4 copy.95
  18.4 2.0 collective-permute-start.1
  20.4 2.2 copy.71
  22.6 19.2 %collective-permute-done = bf16[8,69,1,1024]{3,0,2,1:T(8,128)(2,1)} collective-permute-done((bf16[8,69,1,1024]{3,0,2,1:T(8,128)(2,1)S(1)}, bf16[8,69,1,1024]{3,0,2,1:T(8,128)(2,1)}, u32[]{:S(2)}, u32[]{:S(2)}) %collective-permute-start) | collective-permute-done | bytes 1130528 | tf_op jit(solution)/shard_map/ppermute | solution.py:17
  41.8 1.9 copy.66
  43.7 3.3 collective-permute-done.1
  46.9 1.9 copy.68
  48.9 2.5 pad_maximum_fusion.6
  51.4 73.4 %while.20 = (s32[]{:T(128)}, bf16[8,256,2,1024]{3,1,2,0:T(8,128)(2,1)}, bf16[8,69,4,1024]{3,1,2,0:T(8,128)(2,1)}, bf16[3,3,256,69]{2,3,1,0:T(8,128)(2,1)S(1)}, f32[256]{0:T(256)S(1)}, /*index=5*/s32[]{:T(128)}) while((s32[]{:T(128)}, bf16[8,256,2,1024]{3,1,2,0:T(8,128)(2,1)}, bf16[8,69,4,1024]{3,1,2,0:T(8,128)(2,1)}, ...), condition=%wide.region_1.2_spmd, body=%wide.region_0.1_spmd.sunk | while | flops 661897216 | bytes 47412808 | solution.py:75
  57.7 1.3 fusion.288
  66.9 1.3 fusion.288
  76.0 1.3 fusion.288
  85.2 1.3 fusion.288
  94.3 1.3 fusion.288
  103.5 1.3 fusion.288
  124.8 6.0 fusion.155
  130.8 3.5 collective-permute-start.2
  134.3 4.2 collective-permute-start.3
  138.6 87.3 %collective-permute-done.2 = bf16[8,256,1,1024]{3,1,2,0:T(8,128)(2,1)} collective-permute-done((bf16[8,256,1,1024]{3,1,2,0:T(8,128)(2,1)}, bf16[8,256,1,1024]{3,1,2,0:T(8,128)(2,1)}, u32[]{:S(2)}, u32[]{:S(2)}) %collective-permute-start.2) | collective-permute-done | bytes 4194336 | tf_op jit(solution)/shard_map/ppermute | solution.py:29
  225.9 2.4 collective-permute-done.3
  228.2 76.5 %while.21 = (s32[]{:T(128)}, bf16[8,69,2,1024]{3,1,2,0:T(8,128)(2,1)}, bf16[8,69,2,1024]{3,1,2,0:T(8,128)(2,1)}, bf16[8,256,1,1024]{3,1,2,0:T(8,128)(2,1)}, bf16...) while((s32[]{:T(128)}, ...), condition=%wide.region_3.4_spmd, body=%wide.region_2.3_spmd.sunk | while | flops 675929088 | bytes 41356388 | solution.py:89
  228.2 1.3 dynamic-slice_bitcast_fusion.9
  230.8 1.4 fusion.307
  235.8 2.0 fusion.310
  237.8 1.3 dynamic-slice_bitcast_fusion.9
  240.4 1.4 fusion.307
  245.4 2.0 fusion.310
  247.4 1.3 dynamic-slice_bitcast_fusion.9
  250.0 1.4 fusion.307
  254.9 2.0 fusion.310
  256.9 1.3 dynamic-slice_bitcast_fusion.9
  259.5 1.4 fusion.307
  264.5 2.0 fusion.310
  266.5 1.3 dynamic-slice_bitcast_fusion.9
  269.0 1.4 fusion.307
  274.0 2.0 fusion.310
  276.0 1.3 dynamic-slice_bitcast_fusion.9
  278.6 1.4 fusion.307
  283.6 2.0 fusion.310
  285.6 1.3 dynamic-slice_bitcast_fusion.9
  288.2 1.4 fusion.307
  293.2 2.0 fusion.310
  295.2 1.3 dynamic-slice_bitcast_fusion.9
  297.8 1.4 fusion.307
  302.8 2.0 fusion.310
  304.8 10.9 %copy.73 = bf16[8,69,2,1024]{1,2,0,3:T(2,128)(2,1)} copy(bf16[8,69,2,1024]{3,1,2,0:T(8,128)(2,1)} %get-tuple-element.75) | data formatting | bytes 4521984 | tf_op jit(solution)/shard_map/while | solution.py:89
  315.7 5.0 all-to-all-start
  320.8 48.1 %all-to-all-done = bf16[8,69,2,1024]{1,2,0,3:T(2,128)(2,1)} async-done(((bf16[8,69,2,1024]{1,2,0,3:T(2,128)(2,1)}), bf16[8,69,2,1024]{1,2,0,3:T(2,128)(2,1)}, u32[]{:S(2)}, u32[]{:S(2)}) %all-to-all-start) | async-done | bytes 2261024 | tf_op jit(solution)/shard_map/all_to_all | solution.py:92
  368.9 10.5 %copy.90 = bf16[8,69,2,4,256]{4,3,0,2,1:T(4,128)(2,1)S(1)} copy(bf16[8,69,2,4,256]{1,2,0,4,3:T(2,128)(2,1)} %bitcast.45) | data formatting | bytes 4521984 | tf_op jit(solution)/shard_map/all_to_all | solution.py:92
  379.4 2.7 copy.91
  382.1 3.1 reshape.50
  385.3 159.3 %gather_fusion = bf16[16384]{0:T(1024)(128)(2,1)S(1)} fusion(bf16[2,32,17664]{2,1,0:T(8,128)(2,1)S(1)} %reshape.50, s32[16384]{0:T(1024)S(1)} %bitcast.272), kind=kCustom, calls=%fused_computation | custom fusion | bytes 262144 | tf_op jit(solution)/shard_map/jit(take_along_axis)/gather | solution.py:103
  546.0 16.3 %all-to-all-start.1 = ((f32[128,2,256]{2,1,0:T(2,128)}), f32[128,2,256]{2,1,0:T(2,128)S(1)}, u32[]{:S(2)}, u32[]{:S(2)}) async-start(f32[128,2,256]{2,1,0:T(2,128)} %stack.2), calls=%async_computation.1 | async-start | bytes 524288 | tf_op jit(solution)/shard_map/all_to_all | solution.py:115
  562.5 9.0 all-to-all-done.1
  571.7 350.1 %all-gather = f32[128,2,256]{2,1,0:T(2,128)S(1)} all-gather(f32[1,2,256]{2,1,0:T(2,128)S(1)} %get-tuple-element.172), channel_id=1, replica_groups=mesh['grp'=4,'band'=32] {'grp','band'}, dimensions={0}, use_global_device_ids=true | all-gather | bytes 264192 | tf_op jit(solution)/shard_map/all_gather | solution.py:120
  922.2 2.9 convert_reduce_fusion
  925.2 14.6 %fusion.116 = f32[256,32,32]{2,1,0:T(8,128)S(1)} fusion(f32[256,32,256]{2,1,0:T(8,128)} %all-gather.3.cloned.1.call-done, f32[256,256]{1,0:T(8,128)S(1)} %reshape.51), kind=kOutput, calls=%fused_computation.146 | convolution fusion | flops 807403520 | bytes 9699328 | tf_op jit(solution)/shard_map/pmo,po,pno->pmn/dot_general | solution.py:49
  939.8 4.3 fusion.120
  947.5 9.9 %fusion.131 = f32[256,1,32]{2,1,0:T(1,128)S(1)} fusion(f32[256,32,256]{2,1,0:T(8,128)} %all-gather.3.cloned.1.call-done, f32[256,256,1]{1,0,2:T(8,128)S(1)} %multiply_bitcast_fusion), kind=kOutput, calls=%fused_computation.172 | convolution fusion | flops 25165824 | bytes 8683520 | tf_op jit(solution)/shard_map/pmo,po->pm/dot_general | solution.py:50
  958.1 5.6 convolution_add_fusion.7
  963.7 5.2 reshape.52
  968.9 7.9 copy.80
  (257 shorter events, 110.3 us)
Async XLA Ops:
  13.0 7.4 copy-start
  13.0 28.8 %collective-permute-start = (bf16[8,69,1,1024]{3,0,2,1:T(8,128)(2,1)S(1)}, bf16[8,69,1,1024]{3,0,2,1:T(8,128)(2,1)}, u32[]{:S(2)}, u32[]{:S(2)}) collective-permute-start(bf16[8,69,1,1024]{3,0,2,1:T(8,128)(2,1)S(1)} %copy.94), channel_id=1, source_target_pairs={{0,1},{1,2},{2,3},{3,4},{4,5},{5,6},{6,7},{7,8},{8,9},{9,10},{10,1... | collective-permute-start | bytes 3391496 | tf_op jit(solution)/shard_map/ppermute | solution.py:17
  18.4 28.6 %collective-permute-start.1 = (bf16[8,69,1,1024]{3,0,2,1:T(8,128)(2,1)}, bf16[8,69,1,1024]{3,0,2,1:T(8,128)(2,1)}, u32[]{:S(2)}, u32[]{:S(2)}) collective-permute-start(bf16[8,69,1,1024]{3,0,2,1:T(8,128)(2,1)} %copy.95), channel_id=1, source_target_pairs={{1,0},{2,1},{3,2},{4,3},{5,4},{6,5},{7,6},{8,7},{9,8},{10,9},{11,1... | collective-permute-start | bytes 3391496 | tf_op jit(solution)/shard_map/ppermute | solution.py:19
  22.6 26.2 %copy-start.2 = (bf16[8,69,2,1024]{3,1,2,0:T(8,128)(2,1)S(1)}, bf16[8,69,2,1024]{3,1,2,0:T(8,128)(2,1)}, u32[]{:S(2)}) copy-start(bf16[8,69,2,1024]{3,1,2,0:T(8,128)(2,1)} %copy.71) | copy-start | bytes 6782980
  48.8 2.6 copy-start.3
  48.8 2.5 copy-start.6
  124.8 103.5 %copy-start.4 = (bf16[3,3,69,256]{3,2,1,0:T(8,128)(2,1)S(1)}, bf16[3,3,69,256]{3,2,1,0:T(8,128)(2,1)}, u32[]{:S(2)}) copy-start(bf16[3,3,69,256]{3,2,1,0:T(8,128)(2,1)} %param.17) | copy-start | bytes 953860
  124.8 103.5 %copy-start.11 = (f32[69]{0:T(128)S(1)}, f32[69]{0:T(128)}, u32[]{:S(2)}) copy-start(f32[69]{0:T(128)} %param.18) | copy-start | bytes 832
  130.8 95.0 %collective-permute-start.2 = (bf16[8,256,1,1024]{3,1,2,0:T(8,128)(2,1)}, bf16[8,256,1,1024]{3,1,2,0:T(8,128)(2,1)}, u32[]{:S(2)}, u32[]{:S(2)}) collective-permute-start(bf16[8,256,1,1024]{3,1,2,0:T(8,128)(2,1)} %get-tuple-element.169), channel_id=1, source_target_pairs={{0,1},{1,2},{2,3},{3,4},{4,5},{5,6},{6,7},{7,8},{8,9},{9,10},{10,1... | collective-permute-start | bytes 12582920 | tf_op jit(solution)/shard_map/ppermute | solution.py:29
  134.3 93.9 %collective-permute-start.3 = (bf16[8,256,1,1024]{3,1,2,0:T(8,128)(2,1)}, bf16[8,256,1,1024]{3,1,2,0:T(8,128)(2,1)}, u32[]{:S(2)}, u32[]{:S(2)}) collective-permute-start(bf16[8,256,1,1024]{3,1,2,0:T(8,128)(2,1)} %get-tuple-element.168), channel_id=1, source_target_pairs={{1,0},{2,1},{3,2},{4,3},{5,4},{6,5},{7,6},{8,7},{9,8},{10,9},{11,1... | collective-permute-start | bytes 12582920 | tf_op jit(solution)/shard_map/ppermute | solution.py:29
  315.7 5.1 copy-start.5
  315.7 53.2 %all-to-all-start = ((bf16[8,69,2,1024]{1,2,0,3:T(2,128)(2,1)}), bf16[8,69,2,1024]{1,2,0,3:T(2,128)(2,1)}, u32[]{:S(2)}, u32[]{:S(2)}) async-start(bf16[8,69,2,1024]{1,2,0,3:T(2,128)(2,1)} %copy.73), calls=%async_computation | async-start | bytes 8388608 | tf_op jit(solution)/shard_map/all_to_all | solution.py:92
  320.7 604.5 %all-gather.3.cloned.1.call-start = ((), (), s32[]{:S(2)}) async-start(), calls=%async_computation.2 | async-start | bytes 8454144 | tf_op jit(solution)/shard_map/all_gather | solution.py:113
  379.4 2.7 copy-start.1
  385.2 159.4 %copy-start.7 = (f32[2,256]{1,0:T(2,128)S(1)}, f32[2,256]{1,0:T(2,128)}, u32[]{:S(2)}) copy-start(f32[2,256]{1,0:T(2,128)} %param.21) | copy-start | bytes 6148
  385.2 159.4 %copy-start.8 = (f32[2,256]{1,0:T(2,128)S(1)}, f32[2,256]{1,0:T(2,128)}, u32[]{:S(2)}) copy-start(f32[2,256]{1,0:T(2,128)} %param.20) | copy-start | bytes 6148
  385.2 177.2 %copy-start.9 = (f32[2,8]{1,0:T(2,128)S(1)}, f32[2,8]{1,0:T(2,128)}, u32[]{:S(2)}) copy-start(f32[2,8]{1,0:T(2,128)} %param.23) | copy-start | bytes 196
  385.2 177.2 %copy-start.10 = (s32[2,8]{1,0:T(2,128)S(1)}, s32[2,8]{1,0:T(2,128)}, u32[]{:S(2)}) copy-start(s32[2,8]{1,0:T(2,128)} %param.22) | copy-start | bytes 196
  546.0 25.5 %all-to-all-start.1 = ((f32[128,2,256]{2,1,0:T(2,128)}), f32[128,2,256]{2,1,0:T(2,128)S(1)}, u32[]{:S(2)}, u32[]{:S(2)}) async-start(f32[128,2,256]{2,1,0:T(2,128)} %stack.2), calls=%async_computation.1 | async-start | bytes 524288 | tf_op jit(solution)/shard_map/all_to_all | solution.py:115
Sparse Core Ops, SparseCore 0:
  545.4 322.1 all-gather.2
